TPU v7x, 32 devices: a whole 2x2x4 slice. The times are simulated.
32 devices in a mesh: ep: 16 (over z, x, core), dp: 2 (over y).
Axes of the slice: x: 2, y: 2, z: 4, core: 2. Of those that a mesh axis runs over, the one named last changes fastest.
Arguments:
- tokens: bfloat16 [1024, 4096], P('ep', 'dp'), may hold values from -6 to 6
- expert_ids: int32 [1024, 8], P('ep'), may hold values from 0 to 15, all different within a row
- gate_logits: float32 [1024, 8], P('ep'), may hold values from -6 to 6
- placement: int32 [8], replicated, may hold values from 0 to 15, as said below
- split_rows: int32 [8], replicated, may hold values from 0 to 32
- gate_up_weight: bfloat16 [16, 4096, 2, 1024], P('ep', None, None, 'dp'), may hold values from -0.09375 to 0.09375
- down_weight: bfloat16 [16, 1024, 4096], P('ep', None, 'dp'), may hold values from -0.1875 to 0.1875
- spare_gate_up: bfloat16 [16, 4096, 2, 512], P('ep', None, None, 'dp'), may hold values from -0.09375 to 0.09375
- spare_down: bfloat16 [16, 512, 4096], P('ep', None, 'dp'), may hold values from -0.1875 to 0.1875
Outputs:
- mixed: bfloat16 [1024, 4096], P('ep', 'dp')
Inputs may be any that keep to these rules, and one draw needn't show every extreme that they name: `expert_ids`: each token names 8 different experts. `placement`: 8 different experts.
All inputs are finite; a program needn't handle non-finite values.
Results may differ from a plain program's by a relative error of at most 0.0058.
Values may be sent and summed in bfloat16 or wider, within the bound.
No kernel may reach another device: no remote copies, remote signals or barrier semaphores. Data moves between devices by JAX's collectives and lax.ppermute only.
A program may use at most 64 MiB of HBM per device.

v0:
```python
import jax
import jax.numpy as jnp
from jax import lax
from jax.sharding import PartitionSpec as P


def gate_up(row_block, weight):
    gate_both = jnp.einsum("rd,djf->rjf", row_block, weight, preferred_element_type=jnp.float32)
    return (jax.nn.silu(gate_both[:, 0, :]) * gate_both[:, 1, :]).astype(jnp.bfloat16)


def slot_tables(ids, target, low, limit, capacity, top_count, gate_weight):
    groups, per_group = ids.shape
    group_tokens = per_group // top_count
    hit = ids == target
    ordinal = jnp.arange(per_group, dtype=jnp.int32)
    earlier = (ordinal[None, :] < ordinal[:, None]).astype(jnp.bfloat16)
    rank = jnp.einsum(
        "pq,gq->gp", earlier, hit.astype(jnp.bfloat16), preferred_element_type=jnp.float32
    ).astype(jnp.int32)
    position = rank - low
    kept = hit & (position >= 0) & (position < limit)
    slots = jnp.arange(capacity, dtype=jnp.int32)
    sel = kept[:, :, None] & (position[:, :, None] == slots[None, None, :])
    holds = jnp.any(sel.reshape(groups, group_tokens, top_count, capacity), axis=2)
    pick = jnp.transpose(holds, (0, 2, 1)).astype(jnp.bfloat16)
    scale = jnp.sum(
        jnp.where(kept.reshape(groups * group_tokens, top_count), gate_weight, 0.0), axis=1
    )
    return (pick, holds.astype(jnp.bfloat16), scale)


def side_columns(expert_ids, gate_logits):
    high = gate_logits.astype(jnp.bfloat16)
    rest = gate_logits - high.astype(jnp.float32)
    middle = rest.astype(jnp.bfloat16)
    low = (rest - middle.astype(jnp.float32)).astype(jnp.bfloat16)
    columns = jnp.concatenate([expert_ids.astype(jnp.bfloat16), high, middle, low], axis=1)
    width = -columns.shape[1] % 128
    return jnp.pad(columns, ((0, 0), (0, width)))


def gather_dp(block, axis):
    if lax.axis_size("dp") != 2:
        return lax.all_gather(block, "dp", axis=axis, tiled=True)
    partner = lax.ppermute(block, "dp", perm=[(0, 1), (1, 0)])
    first = lax.axis_index("dp") == 0
    low = jnp.where(first, block, partner)
    high = jnp.where(first, partner, block)
    return jnp.concatenate([low, high], axis=axis)


def down_dp(hidden, weight):
    if lax.axis_size("dp") != 2:
        gathered = lax.all_gather(hidden, "dp", axis=1, tiled=True)
        return jnp.dot(gathered, weight, preferred_element_type=jnp.float32)
    partner = lax.ppermute(hidden, "dp", perm=[(0, 1), (1, 0)])
    blocks = weight.reshape(2, hidden.shape[1], weight.shape[1])
    first = lax.axis_index("dp") == 0
    own = jnp.where(first, blocks[0], blocks[1])
    other = jnp.where(first, blocks[1], blocks[0])
    return jnp.dot(hidden, own, preferred_element_type=jnp.float32) + jnp.dot(
        partner, other, preferred_element_type=jnp.float32
    )


def per_device(
    tokens,
    expert_ids,
    gate_logits,
    placement,
    split_rows,
    gate_up_weight,
    down_weight,
    spare_gate_up,
    spare_down,
):
    ep_count = lax.axis_size("ep")
    me = lax.axis_index("ep")
    group_tokens = tokens.shape[0]
    top_count = expert_ids.shape[1]
    spares = placement.shape[0]
    halves = spare_gate_up.shape[0] * ep_count // spares
    capacity = group_tokens * top_count // ep_count
    per_group = group_tokens * top_count
    d_model = tokens.shape[1] * lax.axis_size("dp")
    whole_rows = gather_dp(tokens, 1)
    packed = jnp.concatenate([whole_rows, side_columns(expert_ids, gate_logits)], axis=1)
    every_row = lax.all_gather(packed, "ep", axis=0, tiled=True)
    all_tokens = every_row.shape[0]
    ids = every_row[:, d_model : d_model + top_count].astype(jnp.int32)
    parts = every_row[:, d_model + top_count : d_model + 4 * top_count].astype(jnp.float32)
    every_logit = (
        parts[:, :top_count] + parts[:, top_count : 2 * top_count] + parts[:, 2 * top_count :]
    )
    ids = ids.reshape(ep_count, per_group)
    gate_score = jax.nn.sigmoid(every_logit)
    gate_weight = 2.5 * gate_score / jnp.sum(gate_score, axis=1, keepdims=True)
    is_match = placement == me
    home_limit = jnp.where(
        jnp.any(is_match),
        jnp.minimum(jnp.sum(jnp.where(is_match, split_rows, 0)), capacity),
        capacity,
    )
    home_pick, home_take, home_scale = slot_tables(
        ids, me, 0, home_limit, capacity, top_count, gate_weight
    )
    spare_index = me // halves
    spare_pick, spare_take, spare_scale = slot_tables(
        ids,
        placement[spare_index],
        split_rows[spare_index],
        capacity,
        capacity,
        top_count,
        gate_weight,
    )
    grouped = every_row.reshape(ep_count, group_tokens, -1)
    slot_rows = ep_count * capacity
    rows = jnp.einsum(
        "gpi,gic->gpc",
        jnp.concatenate([home_pick, spare_pick], axis=1),
        grouped,
        preferred_element_type=jnp.float32,
    ).astype(jnp.bfloat16)
    home_rows = rows[:, :capacity].reshape(slot_rows, -1)
    spare_rows = rows[:, capacity:].reshape(slot_rows, -1)
    home_hidden = gate_up(home_rows[:, :d_model], gate_up_weight[0])
    home_hidden, spare_rows = lax.optimization_barrier((home_hidden, spare_rows))
    home_out = down_dp(home_hidden, down_weight[0])
    home_out = home_out.astype(jnp.bfloat16).reshape(ep_count, capacity, -1)
    spare_out = down_dp(gate_up(spare_rows[:, :d_model], spare_gate_up[0]), spare_down[0])
    spare_high = spare_out.astype(jnp.bfloat16)
    spare_low = (spare_out - spare_high.astype(jnp.float32)).astype(jnp.bfloat16)
    spare_high = spare_high.reshape(ep_count, capacity, -1)
    spare_low = spare_low.reshape(ep_count, capacity, -1)
    home_term = jnp.einsum(
        "gip,gpc->gic", home_take, home_out, preferred_element_type=jnp.float32
    ).reshape(all_tokens, -1)
    spare_term = jnp.einsum(
        "gip,gpc->gic",
        jnp.concatenate([spare_take, spare_take], axis=2),
        jnp.concatenate([spare_high, spare_low], axis=1),
        preferred_element_type=jnp.float32,
    ).reshape(all_tokens, -1)
    partial = home_scale[:, None] * home_term + spare_scale[:, None] * spare_term
    mixed = lax.psum_scatter(partial.astype(jnp.bfloat16), "ep", scatter_dimension=0, tiled=True)
    return mixed.astype(jnp.bfloat16)


def solution(mesh):
    return jax.shard_map(
        per_device,
        mesh=mesh,
        in_specs=(
            P("ep", "dp"),
            P("ep", None),
            P("ep", None),
            P(),
            P(),
            P("ep", None, None, "dp"),
            P("ep", None, "dp"),
            P("ep", None, None, "dp"),
            P("ep", None, "dp"),
        ),
        out_specs=P("ep", "dp"),
        check_vma=False,
    )
```

profile of v0, /device:TPU:0, one launch (start us, length us, event | category | flops | bytes accessed | tf_op | source)
XLA Modules:
  0.0 224.1 jit_solution(15065613179835285331)
XLA Ops:
  6.5 3.0 %collective-permute-start = (bf16[64,2048]{1,0:T(8,128)(2,1)}, bf16[64,2048]{1,0:T(8,128)(2,1)S(1)}, u32[]{:S(2)}, u32[]{:S(2)}) collective-permute-start(bf16[64,2048]{1,0:T(8,128)(2,1)} %param.9), channel_id=1, source_target_pairs={{0,1},{1,0},{2,3},{3,2},{4,5},{5,4},{6,7},{7,6},{8,9},{9,8},{10,11... | collective-permute-start | bytes 786440 | tf_op jit(solution)/shard_map/ppermute | solution.py:46
  9.5 0.7 convert_element_type.75
  10.2 0.8 fusion.67
  11.1 4.9 %collective-permute-done = bf16[64,2048]{1,0:T(8,128)(2,1)S(1)} collective-permute-done((bf16[64,2048]{1,0:T(8,128)(2,1)}, bf16[64,2048]{1,0:T(8,128)(2,1)S(1)}, u32[]{:S(2)}, u32[]{:S(2)}) %collective-permute-start) | collective-permute-done | bytes 262176 | tf_op jit(solution)/shard_map/ppermute | solution.py:46
  16.0 1.0 broadcast_select_fusion.1
  17.0 0.9 fusion.42
  18.0 1.2 dynamic_slice.6
  19.2 1.3 dynamic_slice.7
  20.5 1.4 fusion.59
  22.6 1.4 compare_reduce_fusion
  24.6 71.5 %all-gather.2.cloned.1.call-done = bf16[1024,4224]{1,0:T(8,128)(2,1)} async-done(((bf16[64,4224]{1,0:T(8,128)(2,1)}), bf16[1024,4224]{1,0:T(8,128)(2,1)}) %all-gather.2.cloned.1.call-update) | async-done | bytes 8650768 | tf_op jit(solution)/shard_map/all_gather | solution.py:89
  96.1 1.8 convert_compare_fusion.1
  99.2 0.9 compare_and_fusion
  102.0 5.8 %convolution_convert_fusion = bf16[16,64,4224]{2,1,0:T(8,128)(2,1)S(1)} fusion(bf16[16,64,4224]{2,1,0:T(8,128)(2,1)} %bitcast.84, pred[16,32,64]{2,1,0:T(8,128)(4,1)S(1)} %bitcast.93, pred[16,32,64]{2,1,0:T(8,128)(4,1)S(1)} %bitcast.92), kind=kOutput, calls=%fused_computation | convolution fusion | flops 558039040 | bytes 17367040 | tf_op jit(solution)/shard_map/gpi,gic->gpc/dot_general | solution.py:120
  107.8 0.8 fusion.66
  108.7 7.3 %fusion.2 = f32[512,2,512]{2,0,1:T(8,128)S(1)} fusion(bf16[4096,2,512]{2,1,0:T(2,128)(2,1)} %bitcast.96, bf16[512,4224]{1,0:T(8,128)(2,1)S(1)} %bitcast.89), kind=kOutput, calls=%fused_computation.5 | convolution fusion | flops 4294967296 | bytes 14680064 | tf_op jit(solution)/shard_map/rd,djf->rjf/dot_general | solution.py:8
  115.9 1.1 fusion.30
  117.0 2.3 %fusion.8 = f32[512,2,256]{2,0,1:T(8,128)S(1)} fusion(bf16[4096,2,256]{2,1,0:T(2,128)(2,1)S(1)} %bitcast.97, bf16[512,4224]{1,0:T(8,128)(2,1)S(1)} %bitcast.88), kind=kOutput, calls=%fused_computation.12 | convolution fusion | flops 2147483648 | bytes 9437184 | tf_op jit(solution)/shard_map/rd,djf->rjf/dot_general | solution.py:8
  119.4 0.9 fusion.47
  120.2 1.5 collective-permute-start.2
  121.7 0.5 collective-permute-start.1
  122.3 2.7 %fusion.32 = f32[512,2048]{1,0:T(8,128)} fusion(pred[]{:T(512)S(6)} %eq.61, bf16[1,512,2048]{2,1,0:T(8,128)(2,1)S(1)} %copy-done.1, f32[512,2,256]{2,0,1:T(8,128)S(1)} %fusion.8), kind=kOutput, calls=%fused_computation.46 | convolution fusion | flops 538181632 | bytes 7340033 | tf_op jit(solution)/shard_map/dot_general | solution.py:62
  124.9 4.3 %fusion.13 = f32[512,2048]{1,0:T(8,128)} fusion(bf16[512,512]{1,0:T(8,128)(2,1)} %fusion.30, pred[]{:T(512)S(6)} %eq.61, bf16[1,1024,2048]{2,1,0:T(8,128)(2,1)S(1)} %copy-done.2), kind=kOutput, calls=%fused_computation.20 | convolution fusion | flops 1074790400 | bytes 8912897 | tf_op jit(solution)/shard_map/dot_general | solution.py:62
  129.2 1.1 slice_convert_fusion
  131.7 0.5 select_reduce_fusion.1
  132.3 3.0 %subtract_convert_fusion = (bf16[512,2048]{1,0:T(8,128)(2,1)S(1)}, bf16[512,2048]{1,0:T(8,128)(2,1)S(1)}) fusion(f32[512,2048]{1,0:T(8,128)} %fusion.32, bf16[512,256]{1,0:T(8,128)(2,1)} %collective-permute-done.2, pred[]{:T(512)S(6)} %eq.61, bf16[1,512,2048]{2,1,0:T(8,128)(2,1)S(1)} %copy-done.1), kind=kOutput, calls=%fused_computation.15 | convolution fusion | flops 542638080 | bytes 10747905 | tf_op jit(solution)/shard_map/dot_general | solution.py:62
  135.3 1.6 fusion.4
  136.9 3.2 %collective-permute-done.1 = bf16[512,512]{1,0:T(8,128)(2,1)S(1)} collective-permute-done((bf16[512,512]{1,0:T(8,128)(2,1)}, bf16[512,512]{1,0:T(8,128)(2,1)S(1)}, u32[]{:S(2)}, u32[]{:S(2)}) %collective-permute-start.1) | collective-permute-done | bytes 524320 | tf_op jit(solution)/shard_map/ppermute | solution.py:57
  140.1 1.4 add_convert_fusion
  141.6 1.3 fusion.68
  142.9 3.7 %fusion.1 = bf16[1024,2048]{1,0:T(8,128)(2,1)} fusion(f32[16,64,2048]{2,1,0:T(8,128)S(1)} %fusion.4, f32[16,64,2048]{2,1,0:T(8,128)S(1)} %fusion.68, f32[1024]{0:T(1024)S(1)} %get-tuple-element.10, f32[1024]{0:T(1024)S(1)} %get-tuple-element.9), kind=kLoop, calls=%fused_computation.3 | loop fusion | flops 8388608 | bytes 20979712 | tf_op jit(solution)/shard_map/convert_element_type | solution.py:147
  146.5 70.7 %reduce-scatter.2.cloned.1.call-done = bf16[64,2048]{1,0:T(8,128)(2,1)} async-done(((bf16[1024,2048]{1,0:T(8,128)(2,1)}), bf16[64,2048]{1,0:T(8,128)(2,1)}) %reduce-scatter.2.cloned.1.call-update) | async-done | bytes 262160 | tf_op jit(solution)/shard_map/reduce_scatter | solution.py:147
  (34 shorter events, 4.7 us)
Async XLA Ops:
  6.5 89.6 %all-gather.2.cloned.1.call-start = ((), (), s32[]{:S(2)}) async-start(), calls=%async_computation.1 | async-start | bytes 9191424 | tf_op jit(solution)/shard_map/all_gather | solution.py:89
  6.5 9.5 %collective-permute-start = (bf16[64,2048]{1,0:T(8,128)(2,1)}, bf16[64,2048]{1,0:T(8,128)(2,1)S(1)}, u32[]{:S(2)}, u32[]{:S(2)}) collective-permute-start(bf16[64,2048]{1,0:T(8,128)(2,1)} %param.9), channel_id=1, source_target_pairs={{0,1},{1,0},{2,3},{3,2},{4,5},{5,4},{6,7},{7,6},{8,9},{9,8},{10,11... | collective-permute-start | bytes 786440 | tf_op jit(solution)/shard_map/ppermute | solution.py:46
  17.9 199.3 %reduce-scatter.2.cloned.1.call-start = ((), (), s32[]{:S(2)}) async-start(), calls=%async_computation.2 | async-start | bytes 4456448 | tf_op jit(solution)/shard_map/reduce_scatter | solution.py:147
  108.6 8.4 %copy-start.4 = (bf16[1,4096,2,256]{3,2,1,0:T(2,128)(2,1)S(1)}, bf16[1,4096,2,256]{3,2,1,0:T(2,128)(2,1)}, u32[]{:S(2)}) copy-start(bf16[1,4096,2,256]{3,2,1,0:T(2,128)(2,1)} %param.16) | copy-start | bytes 12582916
  117.0 5.2 %copy-start.1 = (bf16[1,512,2048]{2,1,0:T(8,128)(2,1)S(1)}, bf16[1,512,2048]{2,1,0:T(8,128)(2,1)}, u32[]{:S(2)}) copy-start(bf16[1,512,2048]{2,1,0:T(8,128)(2,1)} %param.17) | copy-start | bytes 6291460
  120.2 4.7 %copy-start.2 = (bf16[1,1024,2048]{2,1,0:T(8,128)(2,1)S(1)}, bf16[1,1024,2048]{2,1,0:T(8,128)(2,1)}, u32[]{:S(2)}) copy-start(bf16[1,1024,2048]{2,1,0:T(8,128)(2,1)} %param.15) | copy-start | bytes 12582916
  120.2 12.0 %collective-permute-start.2 = (bf16[512,256]{1,0:T(8,128)(2,1)}, bf16[512,256]{1,0:T(8,128)(2,1)}, u32[]{:S(2)}, u32[]{:S(2)}) collective-permute-start(bf16[512,256]{1,0:T(8,128)(2,1)} %fusion.47), channel_id=1, source_target_pairs={{0,1},{1,0},{2,3},{3,2},{4,5},{5,4},{6,7},{7,6},{8,9},{9,8},{10,11... | collective-permute-start | bytes 786440 | tf_op jit(solution)/shard_map/ppermute | solution.py:57
  121.7 18.4 %collective-permute-start.1 = (bf16[512,512]{1,0:T(8,128)(2,1)}, bf16[512,512]{1,0:T(8,128)(2,1)S(1)}, u32[]{:S(2)}, u32[]{:S(2)}) collective-permute-start(bf16[512,512]{1,0:T(8,128)(2,1)} %fusion.30), channel_id=1, source_target_pairs={{0,1},{1,0},{2,3},{3,2},{4,5},{5,4},{6,7},{7,6},{8,9},{9,8},{10,11... | collective-permute-start | bytes 1572872 | tf_op jit(solution)/shard_map/ppermute | solution.py:57
  135.3 4.8 %copy-start = (f32[512,2048]{1,0:T(8,128)S(1)}, f32[512,2048]{1,0:T(8,128)}, u32[]{:S(2)}) copy-start(f32[512,2048]{1,0:T(8,128)} %fusion.13) | copy-start | bytes 12582916
  135.3 4.8 %copy-start.3 = (bf16[1,1024,2048]{2,1,0:T(8,128)(2,1)S(1)}, bf16[1,1024,2048]{2,1,0:T(8,128)(2,1)}, u32[]{:S(2)}) copy-start(bf16[1,1024,2048]{2,1,0:T(8,128)(2,1)} %param.15) | copy-start | bytes 12582916
Sparse Core Ops, SparseCore 0:
  18.0 78.0 all-gather.1
  146.7 70.5 reduce-scatter.1
where the time goes:
time: 225 us; the launch traced here: 224 us
  waiting for transfers between devices  150 us (67%)
  matrix products  30.8 us (14%)
  other arithmetic  16.6 us (7%)
  between operations  15.1 us (7%)
  local copies, waits for them, and re-layouts  6.24 us (3%)
  starting transfers between devices  5.04 us (2%)
    all_gather x1, waiting for transfers between devices, per_device(): every_row = lax.all_gather(packed, 'ep', axis=0, tiled=True)  71.5 us
    reduce_scatter x1, waiting for transfers between devices, per_device(): lax.psum_scatter(partial.astype(jnp.bfloat16), 'ep', scatter_dimension=0,...  70.7 us
    dot_general x2, matrix products, gate_up(): jnp.einsum('rd,djf->rjf', row_block, weight, preferred_element_type=jnp.f...  9.58 us
    dot_general x2, matrix products, down_dp(): jnp.dot(hidden, own, preferred_element_type=jnp.float32)  6.95 us
    dot_general x1, matrix products, per_device(): jnp.einsum('gpi,gic->gpc', jnp.concatenate([home_pick, spare_pick], axis=...  5.83 us
    ppermute x1, waiting for transfers between devices, gather_dp(): partner = lax.ppermute(block, 'dp', perm=[(0, 1), (1, 0)])  4.95 us
  transfers between devices with their start and end apart: 5, of which 4 were waited for; matrix products, arithmetic and copies ran while one was open for 10% of the time, Pallas kernels for 0%

commit v1 on v0

--- a/solution.py
+++ b/solution.py
@@ -1,7 +1,35 @@
+import functools
 import jax
 import jax.numpy as jnp
 from jax import lax
 from jax.sharding import PartitionSpec as P
+
+
+def rest_the_indices(page, on_dim):
+    block_now = list(page.shape[1:])
+    block_now[on_dim] *= page.shape[0]
+    return jnp.moveaxis(page, 0, on_dim).reshape(block_now)
+
+
+def seats_all_end(x_local, axis_tag, ndim_at):
+    n_parts = lax.axis_size(axis_tag)
+    found = [(w, (w + 1) % n_parts) for w in range(n_parts)]
+    row_out, s_next = ([], [])
+    kk = 0
+    pages = [(q, dev_i) for dev_i, q in found]
+    while kk < n_parts - 1:
+        if kk % 2 == 0:
+            row_out.append(lax.ppermute(row_out[-1] if row_out else x_local, axis_tag, found))
+        else:
+            s_next.append(lax.ppermute(s_next[-1] if s_next else x_local, axis_tag, pages))
+        kk = kk + 1
+    q_next = jnp.stack([*row_out[::-1], x_local, *s_next], axis=0)
+    base_arr = lax.axis_index(axis_tag) - len(row_out)
+    q_next = q_next[(jnp.arange(n_parts) - base_arr) % n_parts]
+    return rest_the_indices(q_next, ndim_at)
+
+
+page_begin = functools.partial(seats_all_end, axis_tag="ep", ndim_at=0)
 
 
 def gate_up(row_block, weight):
@@ -86,7 +114,7 @@
     d_model = tokens.shape[1] * lax.axis_size("dp")
     whole_rows = gather_dp(tokens, 1)
     packed = jnp.concatenate([whole_rows, side_columns(expert_ids, gate_logits)], axis=1)
-    every_row = lax.all_gather(packed, "ep", axis=0, tiled=True)
+    every_row = page_begin(packed)
     all_tokens = every_row.shape[0]
     ids = every_row[:, d_model : d_model + top_count].astype(jnp.int32)
     parts = every_row[:, d_model + top_count : d_model + 4 * top_count].astype(jnp.float32)

time: 225 us -> 289 us (1.28)
  starting transfers between devices: 5.04 us -> 51 us
  local copies, waits for them, and re-layouts: 6.24 us -> 37 us
  waiting for transfers between devices: 150 us -> 135 us
    all_gather x1 -> x0, waiting for transfers between devices: 71.5 us -> none  [per_device(): every_row = lax.all_gather(packed, 'ep', axis=0, tiled=True)]
    ppermute x0 -> x15, waiting for transfers between devices: none -> 46.7 us  [the longest x8 46.7 us: seats_all_end(): lax.ppermute(row_out[-1] if row_out else x_local, axis_tag, found)]
    ppermute x0 -> x15, starting transfers between devices: none -> 45.8 us  [the longest x8 33.9 us: seats_all_end(): lax.ppermute(row_out[-1] if row_out else x_local, axis_tag, found)]
    unnamed x11 -> x41, local copies, waits for them, and re-layouts: 0.12 us -> 21.8 us
    reduce_scatter x1, waiting for transfers between devices: 70.7 us -> 79.7 us  [per_device(): lax.psum_scatter(partial.astype(jnp.bfloat16), 'ep', scatter_dimension=0,...]
    gather x0 -> x1, local copies, waits for them, and re-layouts: none -> 8.39 us  [seats_all_end(): q_next = q_next[(jnp.arange(n_parts) - base_arr) % n_parts]]
  transfers between devices with their start and end apart: 5 -> 19, of which waited for: 4 -> 10; matrix products, arithmetic and copies ran while one was open for 10% -> 15% of each run, Pallas kernels for 0% -> 0%
where the time goes in v1:
time: 289 us
  waiting for transfers between devices  135 us (47%)
  starting transfers between devices  51 us (18%)
  local copies, waits for them, and re-layouts  37 us (13%)
  matrix products  32 us (11%)
  other arithmetic  17.9 us (6%)
  between operations  15.1 us (5%)
    reduce_scatter x1, waiting for transfers between devices, per_device(): lax.psum_scatter(partial.astype(jnp.bfloat16), 'ep', scatter_dimension=0,...  79.7 us
    ppermute x8, waiting for transfers between devices, seats_all_end(): lax.ppermute(row_out[-1] if row_out else x_local, axis_tag, found)  46.7 us
    ppermute x8, starting transfers between devices, seats_all_end(): lax.ppermute(row_out[-1] if row_out else x_local, axis_tag, found)  33.9 us
    unnamed x41, local copies, waits for them, and re-layouts  21.8 us
    ppermute x7, starting transfers between devices, seats_all_end(): lax.ppermute(s_next[-1] if s_next else x_local, axis_tag, pages)  11.9 us
    dot_general x2, matrix products, gate_up(): jnp.einsum('rd,djf->rjf', row_block, weight, preferred_element_type=jnp.f...  9.78 us
    gather x1, local copies, waits for them, and re-layouts, seats_all_end(): q_next = q_next[(jnp.arange(n_parts) - base_arr) % n_parts]  8.39 us
    dot_general x2, matrix products, down_dp(): jnp.dot(hidden, own, preferred_element_type=jnp.float32)  7.08 us
  transfers between devices with their start and end apart: 19, of which 10 were waited for; matrix products, arithmetic and copies ran while one was open for 15% of the time, Pallas kernels for 0%

profile of v1, /device:TPU:0, one launch (start us, length us, event | category | flops | bytes accessed | tf_op | source)
XLA Modules:
  0.0 288.6 jit_solution(13253713603189057616)
XLA Ops:
  6.5 3.0 %collective-permute-start = (bf16[64,2048]{1,0:T(8,128)(2,1)}, bf16[64,2048]{1,0:T(8,128)(2,1)S(1)}, u32[]{:S(2)}, u32[]{:S(2)}) collective-permute-start(bf16[64,2048]{1,0:T(8,128)(2,1)} %param.9), channel_id=1, source_target_pairs={{0,1},{1,0},{2,3},{3,2},{4,5},{5,4},{6,7},{7,6},{8,9},{9,8},{10,11... | collective-permute-start | bytes 786440 | tf_op jit(solution)/shard_map/ppermute | solution.py:74
  11.1 4.9 %collective-permute-done = bf16[64,2048]{1,0:T(8,128)(2,1)S(1)} collective-permute-done((bf16[64,2048]{1,0:T(8,128)(2,1)}, bf16[64,2048]{1,0:T(8,128)(2,1)S(1)}, u32[]{:S(2)}, u32[]{:S(2)}) %collective-permute-start) | collective-permute-done | bytes 262176 | tf_op jit(solution)/shard_map/ppermute | solution.py:74
  17.1 11.5 %collective-permute-done.1 = bf16[64,4224]{1,0:T(8,128)(2,1)S(1)} collective-permute-done((bf16[64,4224]{1,0:T(8,128)(2,1)S(1)}, bf16[64,4224]{1,0:T(8,128)(2,1)S(1)}, u32[]{:S(2)}, u32[]{:S(2)}) %collective-permute-start.1) | collective-permute-done | bytes 540704 | tf_op jit(solution)/shard_map/ppermute | solution.py:22
  28.6 4.4 %collective-permute-start.9 = (bf16[64,4224]{1,0:T(8,128)(2,1)S(1)}, bf16[64,4224]{1,0:T(8,128)(2,1)S(1)}, u32[]{:S(2)}, u32[]{:S(2)}) collective-permute-start(bf16[64,4224]{1,0:T(8,128)(2,1)S(1)} %fusion.42), channel_id=1, source_target_pairs={{2,0},{4,2},{6,4},{8,6},{10,8},{12,10},{14,12},{16,14},{18,16},{20... | collective-permute-start | bytes 1622024 | tf_op jit(solution)/shard_map/ppermute | solution.py:24
  33.0 7.1 %collective-permute-done.2 = bf16[64,4224]{1,0:T(8,128)(2,1)S(1)} collective-permute-done((bf16[64,4224]{1,0:T(8,128)(2,1)S(1)}, bf16[64,4224]{1,0:T(8,128)(2,1)S(1)}, u32[]{:S(2)}, u32[]{:S(2)}) %collective-permute-start.2) | collective-permute-done | bytes 540704 | tf_op jit(solution)/shard_map/ppermute | solution.py:22
  40.2 4.4 %collective-permute-start.10 = (bf16[64,4224]{1,0:T(8,128)(2,1)S(1)}, bf16[64,4224]{1,0:T(8,128)(2,1)S(1)}, u32[]{:S(2)}, u32[]{:S(2)}) collective-permute-start(bf16[64,4224]{1,0:T(8,128)(2,1)S(1)} %collective-permute-done.9), channel_id=1, source_target_pairs={{2,0},{4,2},{6,4},{8,6},{10,8},{12,10},{14,12},{16,14},{18,16},{20... | collective-permute-start | bytes 1622024 | tf_op jit(solution)/shard_map/ppermute | solution.py:24
  44.6 7.1 %collective-permute-done.3 = bf16[64,4224]{1,0:T(8,128)(2,1)S(1)} collective-permute-done((bf16[64,4224]{1,0:T(8,128)(2,1)S(1)}, bf16[64,4224]{1,0:T(8,128)(2,1)S(1)}, u32[]{:S(2)}, u32[]{:S(2)}) %collective-permute-start.3) | collective-permute-done | bytes 540704 | tf_op jit(solution)/shard_map/ppermute | solution.py:22
  53.6 2.6 collective-permute-start.11
  56.2 7.1 %collective-permute-done.4 = bf16[64,4224]{1,0:T(8,128)(2,1)S(1)} collective-permute-done((bf16[64,4224]{1,0:T(8,128)(2,1)S(1)}, bf16[64,4224]{1,0:T(8,128)(2,1)S(1)}, u32[]{:S(2)}, u32[]{:S(2)}) %collective-permute-start.4) | collective-permute-done | bytes 540704 | tf_op jit(solution)/shard_map/ppermute | solution.py:22
  63.3 4.1 %collective-permute-start.5 = (bf16[64,4224]{1,0:T(8,128)(2,1)S(1)}, bf16[64,4224]{1,0:T(8,128)(2,1)S(1)}, u32[]{:S(2)}, u32[]{:S(2)}) collective-permute-start(bf16[64,4224]{1,0:T(8,128)(2,1)S(1)} %collective-permute-done.4), channel_id=1, source_target_pairs={{0,2},{2,4},{4,6},{6,8},{8,10},{10,12},{12,14},{14,16},{16,18},{18... | collective-permute-start | bytes 1622024 | tf_op jit(solution)/shard_map/ppermute | solution.py:22
  68.6 6.3 %collective-permute-done.5 = bf16[64,4224]{1,0:T(8,128)(2,1)S(1)} collective-permute-done((bf16[64,4224]{1,0:T(8,128)(2,1)S(1)}, bf16[64,4224]{1,0:T(8,128)(2,1)S(1)}, u32[]{:S(2)}, u32[]{:S(2)}) %collective-permute-start.5) | collective-permute-done | bytes 540704 | tf_op jit(solution)/shard_map/ppermute | solution.py:22
  74.9 7.1 %collective-permute-start.6 = (bf16[64,4224]{1,0:T(8,128)(2,1)S(1)}, bf16[64,4224]{1,0:T(8,128)(2,1)S(1)}, u32[]{:S(2)}, u32[]{:S(2)}) collective-permute-start(bf16[64,4224]{1,0:T(8,128)(2,1)S(1)} %collective-permute-done.5), channel_id=1, source_target_pairs={{0,2},{2,4},{4,6},{6,8},{8,10},{10,12},{12,14},{14,16},{16,18},{18... | collective-permute-start | bytes 1622024 | tf_op jit(solution)/shard_map/ppermute | solution.py:22
  82.8 3.6 %collective-permute-done.6 = bf16[64,4224]{1,0:T(8,128)(2,1)S(1)} collective-permute-done((bf16[64,4224]{1,0:T(8,128)(2,1)S(1)}, bf16[64,4224]{1,0:T(8,128)(2,1)S(1)}, u32[]{:S(2)}, u32[]{:S(2)}) %collective-permute-start.6) | collective-permute-done | bytes 540704 | tf_op jit(solution)/shard_map/ppermute | solution.py:22
  86.4 10.2 %collective-permute-start.7 = (bf16[64,4224]{1,0:T(8,128)(2,1)S(1)}, bf16[64,4224]{1,0:T(8,128)(2,1)}, u32[]{:S(2)}, u32[]{:S(2)}) collective-permute-start(bf16[64,4224]{1,0:T(8,128)(2,1)S(1)} %collective-permute-done.6), channel_id=1, source_target_pairs={{0,2},{2,4},{4,6},{6,8},{8,10},{10,12},{12,14},{14,16},{16,18},{18... | collective-permute-start | bytes 1622024 | tf_op jit(solution)/shard_map/ppermute | solution.py:22
  96.6 3.9 %collective-permute-done.7 = bf16[64,4224]{1,0:T(8,128)(2,1)} collective-permute-done((bf16[64,4224]{1,0:T(8,128)(2,1)S(1)}, bf16[64,4224]{1,0:T(8,128)(2,1)}, u32[]{:S(2)}, u32[]{:S(2)}) %collective-permute-start.7) | collective-permute-done | bytes 540704 | tf_op jit(solution)/shard_map/ppermute | solution.py:22
  100.5 10.7 %collective-permute-start.8 = (bf16[64,4224]{1,0:T(8,128)(2,1)}, bf16[64,4224]{1,0:T(8,128)(2,1)}, u32[]{:S(2)}, u32[]{:S(2)}) collective-permute-start(bf16[64,4224]{1,0:T(8,128)(2,1)} %collective-permute-done.7), channel_id=1, source_target_pairs={{0,2},{2,4},{4,6},{6,8},{8,10},{10,12},{12,14},{14,16},{16,18},{18... | collective-permute-start | bytes 1622024 | tf_op jit(solution)/shard_map/ppermute | solution.py:22
  118.0 1.9 bitcast_dynamic-update-slice_fusion.15
  119.9 1.9 bitcast_dynamic-update-slice_fusion.14
  121.8 1.9 bitcast_dynamic-update-slice_fusion.13
  123.7 2.0 bitcast_dynamic-update-slice_fusion.12
  135.1 1.9 bitcast_dynamic-update-slice_fusion.1
  137.9 8.4 %gather_fusion = bf16[16,64,4224]{2,1,0:T(8,128)(2,1)} fusion(bf16[16,64,4224]{2,1,0:T(8,128)(2,1)} %bitcast_dynamic-update-slice_fusion, s32[1024]{0:T(1024)S(1)} %pad_clamp_fusion), kind=kCustom, calls=%fused_computation | custom fusion | bytes 17301568 | tf_op jit(solution)/shard_map/gather | solution.py:28
  153.3 5.8 %convolution_convert_fusion = bf16[16,64,4224]{2,1,0:T(8,128)(2,1)S(1)} fusion(bf16[16,64,4224]{2,1,0:T(8,128)(2,1)} %gather_fusion, pred[16,32,64]{2,1,0:T(8,128)(4,1)S(1)} %bitcast.128, pred[16,32,64]{2,1,0:T(8,128)(4,1)S(1)} %bitcast.127), kind=kOutput, calls=%fused_computation.1 | convolution fusion | flops 558039040 | bytes 17367040 | tf_op jit(solution)/shard_map/gpi,gic->gpc/dot_general | solution.py:148
  159.8 7.4 %fusion.2 = f32[512,2,512]{2,0,1:T(8,128)S(1)} fusion(bf16[4096,2,512]{2,1,0:T(2,128)(2,1)} %bitcast.131, bf16[512,4224]{1,0:T(8,128)(2,1)S(1)} %bitcast.124), kind=kOutput, calls=%fused_computation.6 | convolution fusion | flops 4294967296 | bytes 14680064 | tf_op jit(solution)/shard_map/rd,djf->rjf/dot_general | solution.py:36
  169.9 4.3 %fusion.13 = f32[512,2048]{1,0:T(8,128)} fusion(bf16[512,512]{1,0:T(8,128)(2,1)} %fusion.30, pred[]{:T(512)S(6)} %eq.63, bf16[1,1024,2048]{2,1,0:T(8,128)(2,1)S(1)} %copy-done.2), kind=kOutput, calls=%fused_computation.21 | convolution fusion | flops 1074790400 | bytes 8912897 | tf_op jit(solution)/shard_map/dot_general | solution.py:90
  174.2 2.3 fusion.8
  177.4 2.7 fusion.32
  184.1 4.1 %collective-permute-done.17 = bf16[512,256]{1,0:T(8,128)(2,1)S(1)} collective-permute-done((bf16[512,256]{1,0:T(8,128)(2,1)}, bf16[512,256]{1,0:T(8,128)(2,1)S(1)}, u32[]{:S(2)}, u32[]{:S(2)}) %collective-permute-start.17) | collective-permute-done | bytes 262176 | tf_op jit(solution)/shard_map/ppermute | solution.py:85
  188.2 2.9 %subtract_convert_fusion = (bf16[512,2048]{1,0:T(8,128)(2,1)S(1)}, bf16[512,2048]{1,0:T(8,128)(2,1)S(1)}) fusion(f32[512,2048]{1,0:T(8,128)} %fusion.32, bf16[512,256]{1,0:T(8,128)(2,1)S(1)} %collective-permute-done.17, pred[]{:T(512)S(6)} %eq.63, bf16[1,512,2048]{2,1,0:T(8,128)(2,1)S(1)} %copy-done.1), kind=kOutput, calls=%fused_computation.16 | convolution fusion | flops 542638080 | bytes 10747905 | tf_op jit(solution)/shard_map/dot_general | solution.py:90
  194.6 2.4 add_convert_fusion
  198.3 3.7 %fusion.1 = bf16[1024,2048]{1,0:T(8,128)(2,1)} fusion(f32[16,64,2048]{2,1,0:T(8,128)S(1)} %fusion.4, f32[16,64,2048]{2,1,0:T(8,128)S(1)} %fusion.70, f32[1024]{0:T(1024)S(1)} %get-tuple-element.10, f32[1024]{0:T(1024)S(1)} %get-tuple-element.9), kind=kLoop, calls=%fused_computation.4 | loop fusion | flops 8388608 | bytes 20979712 | tf_op jit(solution)/shard_map/convert_element_type | solution.py:175
  202.0 79.7 %reduce-scatter.2.cloned.1.call-done = bf16[64,2048]{1,0:T(8,128)(2,1)} async-done(((bf16[1024,2048]{1,0:T(8,128)(2,1)}), bf16[64,2048]{1,0:T(8,128)(2,1)}) %reduce-scatter.2.cloned.1.call-update) | async-done | bytes 262160 | tf_op jit(solution)/shard_map/reduce_scatter | solution.py:175
  (96 shorter events, 42.0 us)
Async XLA Ops:
  6.5 275.2 %reduce-scatter.2.cloned.1.call-start = ((), (), s32[]{:S(2)}) async-start(), calls=%async_computation.1 | async-start | bytes 4456448 | tf_op jit(solution)/shard_map/reduce_scatter | solution.py:175
  6.5 9.5 %collective-permute-start = (bf16[64,2048]{1,0:T(8,128)(2,1)}, bf16[64,2048]{1,0:T(8,128)(2,1)S(1)}, u32[]{:S(2)}, u32[]{:S(2)}) collective-permute-start(bf16[64,2048]{1,0:T(8,128)(2,1)} %param.9), channel_id=1, source_target_pairs={{0,1},{1,0},{2,3},{3,2},{4,5},{5,4},{6,7},{7,6},{8,9},{9,8},{10,11... | collective-permute-start | bytes 786440 | tf_op jit(solution)/shard_map/ppermute | solution.py:74
  17.1 11.5 %collective-permute-start.1 = (bf16[64,4224]{1,0:T(8,128)(2,1)S(1)}, bf16[64,4224]{1,0:T(8,128)(2,1)S(1)}, u32[]{:S(2)}, u32[]{:S(2)}) collective-permute-start(bf16[64,4224]{1,0:T(8,128)(2,1)S(1)} %fusion.42), channel_id=1, source_target_pairs={{0,2},{2,4},{4,6},{6,8},{8,10},{10,12},{12,14},{14,16},{16,18},{18... | collective-permute-start | bytes 1622024 | tf_op jit(solution)/shard_map/ppermute | solution.py:22
  28.6 11.6 %collective-permute-start.2 = (bf16[64,4224]{1,0:T(8,128)(2,1)S(1)}, bf16[64,4224]{1,0:T(8,128)(2,1)S(1)}, u32[]{:S(2)}, u32[]{:S(2)}) collective-permute-start(bf16[64,4224]{1,0:T(8,128)(2,1)S(1)} %collective-permute-done.1), channel_id=1, source_target_pairs={{0,2},{2,4},{4,6},{6,8},{8,10},{10,12},{12,14},{14,16},{16,18},{18... | collective-permute-start | bytes 1622024 | tf_op jit(solution)/shard_map/ppermute | solution.py:22
  28.6 11.6 %collective-permute-start.9 = (bf16[64,4224]{1,0:T(8,128)(2,1)S(1)}, bf16[64,4224]{1,0:T(8,128)(2,1)S(1)}, u32[]{:S(2)}, u32[]{:S(2)}) collective-permute-start(bf16[64,4224]{1,0:T(8,128)(2,1)S(1)} %fusion.42), channel_id=1, source_target_pairs={{2,0},{4,2},{6,4},{8,6},{10,8},{12,10},{14,12},{16,14},{18,16},{20... | collective-permute-start | bytes 1622024 | tf_op jit(solution)/shard_map/ppermute | solution.py:24
  40.2 11.6 %collective-permute-start.3 = (bf16[64,4224]{1,0:T(8,128)(2,1)S(1)}, bf16[64,4224]{1,0:T(8,128)(2,1)S(1)}, u32[]{:S(2)}, u32[]{:S(2)}) collective-permute-start(bf16[64,4224]{1,0:T(8,128)(2,1)S(1)} %collective-permute-done.2), channel_id=1, source_target_pairs={{0,2},{2,4},{4,6},{6,8},{8,10},{10,12},{12,14},{14,16},{16,18},{18... | collective-permute-start | bytes 1622024 | tf_op jit(solution)/shard_map/ppermute | solution.py:22
  40.2 13.4 %collective-permute-start.10 = (bf16[64,4224]{1,0:T(8,128)(2,1)S(1)}, bf16[64,4224]{1,0:T(8,128)(2,1)S(1)}, u32[]{:S(2)}, u32[]{:S(2)}) collective-permute-start(bf16[64,4224]{1,0:T(8,128)(2,1)S(1)} %collective-permute-done.9), channel_id=1, source_target_pairs={{2,0},{4,2},{6,4},{8,6},{10,8},{12,10},{14,12},{16,14},{18,16},{20... | collective-permute-start | bytes 1622024 | tf_op jit(solution)/shard_map/ppermute | solution.py:24
  51.8 11.6 %collective-permute-start.4 = (bf16[64,4224]{1,0:T(8,128)(2,1)S(1)}, bf16[64,4224]{1,0:T(8,128)(2,1)S(1)}, u32[]{:S(2)}, u32[]{:S(2)}) collective-permute-start(bf16[64,4224]{1,0:T(8,128)(2,1)S(1)} %collective-permute-done.3), channel_id=1, source_target_pairs={{0,2},{2,4},{4,6},{6,8},{8,10},{10,12},{12,14},{14,16},{16,18},{18... | collective-permute-start | bytes 1622024 | tf_op jit(solution)/shard_map/ppermute | solution.py:22
  53.6 13.8 %collective-permute-start.11 = (bf16[64,4224]{1,0:T(8,128)(2,1)S(1)}, bf16[64,4224]{1,0:T(8,128)(2,1)S(1)}, u32[]{:S(2)}, u32[]{:S(2)}) collective-permute-start(bf16[64,4224]{1,0:T(8,128)(2,1)S(1)} %collective-permute-done.10), channel_id=1, source_target_pairs={{2,0},{4,2},{6,4},{8,6},{10,8},{12,10},{14,12},{16,14},{18,16},{20... | collective-permute-start | bytes 1622024 | tf_op jit(solution)/shard_map/ppermute | solution.py:24
  63.3 33.3 %copy-start.8 = (bf16[64,4224]{1,0:T(8,128)(2,1)}, bf16[64,4224]{1,0:T(8,128)(2,1)S(1)}, u32[]{:S(2)}) copy-start(bf16[64,4224]{1,0:T(8,128)(2,1)S(1)} %collective-permute-done.4) | copy-start | bytes 1622020
  63.3 11.6 %collective-permute-start.5 = (bf16[64,4224]{1,0:T(8,128)(2,1)S(1)}, bf16[64,4224]{1,0:T(8,128)(2,1)S(1)}, u32[]{:S(2)}, u32[]{:S(2)}) collective-permute-start(bf16[64,4224]{1,0:T(8,128)(2,1)S(1)} %collective-permute-done.4), channel_id=1, source_target_pairs={{0,2},{2,4},{4,6},{6,8},{8,10},{10,12},{12,14},{14,16},{16,18},{18... | collective-permute-start | bytes 1622024 | tf_op jit(solution)/shard_map/ppermute | solution.py:22
  67.4 0.8 copy-start.4
  68.3 13.7 %collective-permute-start.12 = (bf16[64,4224]{1,0:T(8,128)(2,1)S(1)}, bf16[64,4224]{1,0:T(8,128)(2,1)S(1)}, u32[]{:S(2)}, u32[]{:S(2)}) collective-permute-start(bf16[64,4224]{1,0:T(8,128)(2,1)S(1)} %collective-permute-done.11), channel_id=1, source_target_pairs={{2,0},{4,2},{6,4},{8,6},{10,8},{12,10},{14,12},{16,14},{18,16},{20... | collective-permute-start | bytes 1622024 | tf_op jit(solution)/shard_map/ppermute | solution.py:24
  74.9 21.7 %copy-start.10 = (bf16[64,4224]{1,0:T(8,128)(2,1)}, bf16[64,4224]{1,0:T(8,128)(2,1)S(1)}, u32[]{:S(2)}) copy-start(bf16[64,4224]{1,0:T(8,128)(2,1)S(1)} %collective-permute-done.5) | copy-start | bytes 1622020
  74.9 11.5 %collective-permute-start.6 = (bf16[64,4224]{1,0:T(8,128)(2,1)S(1)}, bf16[64,4224]{1,0:T(8,128)(2,1)S(1)}, u32[]{:S(2)}, u32[]{:S(2)}) collective-permute-start(bf16[64,4224]{1,0:T(8,128)(2,1)S(1)} %collective-permute-done.5), channel_id=1, source_target_pairs={{0,2},{2,4},{4,6},{6,8},{8,10},{10,12},{12,14},{14,16},{16,18},{18... | collective-permute-start | bytes 1622024 | tf_op jit(solution)/shard_map/ppermute | solution.py:22
  82.0 0.8 copy-start.6
  82.8 13.8 %collective-permute-start.13 = (bf16[64,4224]{1,0:T(8,128)(2,1)S(1)}, bf16[64,4224]{1,0:T(8,128)(2,1)}, u32[]{:S(2)}, u32[]{:S(2)}) collective-permute-start(bf16[64,4224]{1,0:T(8,128)(2,1)S(1)} %collective-permute-done.12), channel_id=1, source_target_pairs={{2,0},{4,2},{6,4},{8,6},{10,8},{12,10},{14,12},{16,14},{18,16},{20... | collective-permute-start | bytes 1622024 | tf_op jit(solution)/shard_map/ppermute | solution.py:24
  86.4 14.1 %copy-start.11 = (bf16[64,4224]{1,0:T(8,128)(2,1)}, bf16[64,4224]{1,0:T(8,128)(2,1)S(1)}, u32[]{:S(2)}) copy-start(bf16[64,4224]{1,0:T(8,128)(2,1)S(1)} %collective-permute-done.6) | copy-start | bytes 1622020
  86.4 14.1 %collective-permute-start.7 = (bf16[64,4224]{1,0:T(8,128)(2,1)S(1)}, bf16[64,4224]{1,0:T(8,128)(2,1)}, u32[]{:S(2)}, u32[]{:S(2)}) collective-permute-start(bf16[64,4224]{1,0:T(8,128)(2,1)S(1)} %collective-permute-done.6), channel_id=1, source_target_pairs={{0,2},{2,4},{4,6},{6,8},{8,10},{10,12},{12,14},{14,16},{16,18},{18... | collective-permute-start | bytes 1622024 | tf_op jit(solution)/shard_map/ppermute | solution.py:22
  96.6 21.3 %collective-permute-start.14 = (bf16[64,4224]{1,0:T(8,128)(2,1)}, bf16[64,4224]{1,0:T(8,128)(2,1)}, u32[]{:S(2)}, u32[]{:S(2)}) collective-permute-start(bf16[64,4224]{1,0:T(8,128)(2,1)} %collective-permute-done.13), channel_id=1, source_target_pairs={{2,0},{4,2},{6,4},{8,6},{10,8},{12,10},{14,12},{16,14},{18,16},{20... | collective-permute-start | bytes 1622024 | tf_op jit(solution)/shard_map/ppermute | solution.py:24
  100.5 17.5 %collective-permute-start.8 = (bf16[64,4224]{1,0:T(8,128)(2,1)}, bf16[64,4224]{1,0:T(8,128)(2,1)}, u32[]{:S(2)}, u32[]{:S(2)}) collective-permute-start(bf16[64,4224]{1,0:T(8,128)(2,1)} %collective-permute-done.7), channel_id=1, source_target_pairs={{0,2},{2,4},{4,6},{6,8},{8,10},{10,12},{12,14},{14,16},{16,18},{18... | collective-permute-start | bytes 1622024 | tf_op jit(solution)/shard_map/ppermute | solution.py:22
  117.9 7.8 %copy-start.9 = (bf16[64,4224]{1,0:T(8,128)(2,1)S(1)}, bf16[64,4224]{1,0:T(8,128)(2,1)}, u32[]{:S(2)}) copy-start(bf16[64,4224]{1,0:T(8,128)(2,1)} %copy-done.8) | copy-start | bytes 1622020
  117.9 19.1 %collective-permute-start.15 = (bf16[64,4224]{1,0:T(8,128)(2,1)}, bf16[64,4224]{1,0:T(8,128)(2,1)S(1)}, u32[]{:S(2)}, u32[]{:S(2)}) collective-permute-start(bf16[64,4224]{1,0:T(8,128)(2,1)} %collective-permute-done.14), channel_id=1, source_target_pairs={{2,0},{4,2},{6,4},{8,6},{10,8},{12,10},{14,12},{16,14},{18,16},{20... | collective-permute-start | bytes 1622024 | tf_op jit(solution)/shard_map/ppermute | solution.py:24
  123.7 7.9 %copy-start.5 = (bf16[64,4224]{1,0:T(8,128)(2,1)S(1)}, bf16[64,4224]{1,0:T(8,128)(2,1)}, u32[]{:S(2)}) copy-start(bf16[64,4224]{1,0:T(8,128)(2,1)} %copy-done.4) | copy-start | bytes 1622020
  125.6 6.7 %copy-start.7 = (bf16[64,4224]{1,0:T(8,128)(2,1)S(1)}, bf16[64,4224]{1,0:T(8,128)(2,1)}, u32[]{:S(2)}) copy-start(bf16[64,4224]{1,0:T(8,128)(2,1)} %copy-done.6) | copy-start | bytes 1622020
  159.8 10.1 %copy-start.2 = (bf16[1,1024,2048]{2,1,0:T(8,128)(2,1)S(1)}, bf16[1,1024,2048]{2,1,0:T(8,128)(2,1)}, u32[]{:S(2)}) copy-start(bf16[1,1024,2048]{2,1,0:T(8,128)(2,1)} %param.15) | copy-start | bytes 12582916
  168.4 5.9 %copy-start.12 = (bf16[1,4096,2,256]{3,2,1,0:T(2,128)(2,1)S(1)}, bf16[1,4096,2,256]{3,2,1,0:T(2,128)(2,1)}, u32[]{:S(2)}) copy-start(bf16[1,4096,2,256]{3,2,1,0:T(2,128)(2,1)} %param.16) | copy-start | bytes 12582916
  168.4 24.3 %collective-permute-start.16 = (bf16[512,512]{1,0:T(8,128)(2,1)}, bf16[512,512]{1,0:T(8,128)(2,1)}, u32[]{:S(2)}, u32[]{:S(2)}) collective-permute-start(bf16[512,512]{1,0:T(8,128)(2,1)} %fusion.30), channel_id=1, source_target_pairs={{0,1},{1,0},{2,3},{3,2},{4,5},{5,4},{6,7},{7,6},{8,9},{9,8},{10,11... | collective-permute-start | bytes 1572872 | tf_op jit(solution)/shard_map/ppermute | solution.py:85
  174.2 3.2 %copy-start.1 = (bf16[1,512,2048]{2,1,0:T(8,128)(2,1)S(1)}, bf16[1,512,2048]{2,1,0:T(8,128)(2,1)}, u32[]{:S(2)}) copy-start(bf16[1,512,2048]{2,1,0:T(8,128)(2,1)} %param.17) | copy-start | bytes 6291460
  180.2 8.0 %collective-permute-start.17 = (bf16[512,256]{1,0:T(8,128)(2,1)}, bf16[512,256]{1,0:T(8,128)(2,1)S(1)}, u32[]{:S(2)}, u32[]{:S(2)}) collective-permute-start(bf16[512,256]{1,0:T(8,128)(2,1)} %fusion.47), channel_id=1, source_target_pairs={{0,1},{1,0},{2,3},{3,2},{4,5},{5,4},{6,7},{7,6},{8,9},{9,8},{10,11... | collective-permute-start | bytes 786440 | tf_op jit(solution)/shard_map/ppermute | solution.py:85
  191.1 2.2 copy-start
  191.1 3.5 %copy-start.3 = (bf16[1,1024,2048]{2,1,0:T(8,128)(2,1)S(1)}, bf16[1,1024,2048]{2,1,0:T(8,128)(2,1)}, u32[]{:S(2)}) copy-start(bf16[1,1024,2048]{2,1,0:T(8,128)(2,1)} %param.15) | copy-start | bytes 12582916
Sparse Core Ops, SparseCore 0:
  202.1 79.5 reduce-scatter.1
